TPU v7x, 256 devices: a whole 4x4x8 slice. The times are simulated.
256 devices in a mesh: in: 4 (over x), out: 64 (over z, y, core).
Axes of the slice: x: 4, y: 4, z: 8, core: 2. Of those that a mesh axis runs over, the one named last changes fastest.
Arguments:
- activations: bfloat16 [8192, 4096], P('out', 'in'), may hold values from -6 to 6
- out_grad: bfloat16 [8192, 16384], P('in', 'out'), may hold values from -0.06591797 to 0.06591797
- block_rows: int32 [4, 64, 4], P('in', 'out'), may hold values from 0 to 31, as said below
- block_cols: int32 [4, 64, 4], P('in', 'out'), may hold values from 0 to 127, as said below
- counts: int32 [4, 64], P('in', 'out'), may hold values from 1 to 4, as said below
Outputs:
- grad_blocks: float32 [4, 64, 4, 128, 128], P('in', 'out')
Inputs may be any that keep to these rules, and one draw needn't show every extreme that they name: `block_rows`: tile (i, j) lists blocks of its own region only: rows i * 8 to (i + 1) * 8 - 1; slots of one tile name different blocks, and slots past counts[i, j] also name blocks of the tile. `block_cols`: columns j * 2 to (j + 1) * 2 - 1 for tile (i, j). `counts`: some tile has a full list in every draw.
All inputs are finite; a program needn't handle non-finite values.
Results may differ from a plain program's by a relative error of at most 0.0003.
Values may be sent and summed in bfloat16 or wider, within the bound.
No kernel may reach another device: no remote copies, remote signals or barrier semaphores. Data moves between devices by JAX's collectives and lax.ppermute only.
A program may use at most 128 MiB of HBM per device.

v0:
```python
import jax
import jax.numpy as jnp
from jax import lax
from jax.sharding import PartitionSpec as P

BLK = 128
MAXB = 4


def block_products(left_rows, grad_rows, local_cols, tile_cols):
    width = grad_rows.shape[0]
    right = jnp.take(grad_rows.reshape(width, tile_cols, BLK), local_cols, axis=1)
    return jnp.einsum("nbi,nbj->bij", left_rows, right, preferred_element_type=jnp.float32)


def on_device(activations, out_grad, block_rows, block_cols, counts):
    in_place = lax.axis_index("in")
    out_place = lax.axis_index("out")
    tile_rows = activations.shape[1] // BLK
    tile_cols = out_grad.shape[1] // BLK
    local_rows = block_rows[0, 0] - in_place * tile_rows
    local_cols = block_cols[0, 0] - out_place * tile_cols
    live = counts[0, 0]
    grad_all = lax.all_gather(out_grad, "in", axis=0, tiled=True)
    piece = lax.all_gather(activations, "out", axis=0, tiled=True)
    height = piece.shape[0]
    left = jnp.take(piece.reshape(height, tile_rows, BLK), local_rows, axis=1)
    totals = block_products(left, grad_all, local_cols, tile_cols)
    keep = (jnp.arange(MAXB, dtype=jnp.int32) < live)[:, None, None]
    result = jnp.where(keep, totals, jnp.zeros_like(totals))
    return result.reshape(1, 1, MAXB, BLK, BLK)


def solution(mesh):
    return jax.shard_map(
        on_device,
        mesh=mesh,
        in_specs=(
            P("out", "in"),
            P("in", "out"),
            P("in", "out", None),
            P("in", "out", None),
            P("in", "out"),
        ),
        out_specs=P("in", "out", None, None, None),
        check_vma=False,
    )
```

profile of v0, /device:TPU:1, one launch (start us, length us, event | category | flops | bytes accessed | tf_op | source)
XLA Modules:
  0.0 228.5 jit_solution(16223086437838721816)
XLA Ops:
  6.5 0.0 all-gather.5.cloned.1.call-start
  6.5 0.7 all-gather.5.cloned.1.call-update
  7.3 0.0 all-gather.3.cloned.1.call-start
  7.3 0.7 all-gather.3.cloned.1.call-update
  8.7 0.7 fusion.11
  9.3 0.7 fusion.10
  10.0 0.7 compare_and_fusion
  10.7 52.8 %all-gather.5.cloned.1.call-done = bf16[8192,256]{1,0:T(8,128)(2,1)} async-done(((bf16[2048,256]{1,0:T(8,128)(2,1)}), bf16[8192,256]{1,0:T(8,128)(2,1)}) %all-gather.5.cloned.1.call-update) | async-done | bytes 4194320 | tf_op jit(solution)/shard_map/all_gather | solution.py:24
  63.5 4.5 %fusion.15 = (bf16[4096,256]{1,0:T(8,128)(2,1)}, bf16[4096,256]{1,0:T(8,128)(2,1)}) fusion(bf16[8192,256]{1,0:T(8,128)(2,1)} %all-gather.5.cloned.1.call-done), kind=kLoop, calls=%fused_computation.30 | loop fusion | bytes 8388608 | tf_op jit(solution)/shard_map/jit(_take)/gather | solution.py:12
  68.0 2.9 %copy.9 = bf16[4096,256]{0,1:T(8,128)(2,1)S(1)} copy(bf16[4096,256]{1,0:T(8,128)(2,1)} %get-tuple-element.7) | data formatting | bytes 4194304 | tf_op jit(solution)/shard_map/jit(_take)/gather | solution.py:12
  70.9 4.1 %copy.10 = bf16[4096,256]{0,1:T(8,128)(2,1)} copy(bf16[4096,256]{1,0:T(8,128)(2,1)} %get-tuple-element.8) | data formatting | bytes 4194304 | tf_op jit(solution)/shard_map/jit(_take)/gather | solution.py:12
  75.0 2.8 %gather_fusion.2 = bf16[4,4096,128]{1,2,0:T(8,128)(2,1)} fusion(bf16[4096,2,128]{0,2,1:T(8,128)(2,1)S(1)} %bitcast.26, s32[1024]{0:T(1024)S(1)} %pad_clamp_fusion), kind=kCustom, calls=%fused_computation.2 | custom fusion | bytes 8388624 | tf_op jit(solution)/shard_map/jit(_take)/gather | solution.py:12
  77.8 4.6 %gather_fusion.3 = bf16[4,4096,128]{1,2,0:T(8,128)(2,1)} fusion(bf16[4096,2,128]{0,2,1:T(8,128)(2,1)} %bitcast.27, s32[1024]{0:T(1024)S(1)} %pad_clamp_fusion), kind=kCustom, calls=%fused_computation.3 | custom fusion | bytes 8388624 | tf_op jit(solution)/shard_map/jit(_take)/gather | solution.py:12
  82.4 84.2 %all-gather.3.cloned.1.call-done = bf16[8192,1024]{1,0:T(8,128)(2,1)} async-done(((bf16[128,1024]{1,0:T(8,128)(2,1)}), bf16[8192,1024]{1,0:T(8,128)(2,1)}) %all-gather.3.cloned.1.call-update) | async-done | bytes 16777232 | tf_op jit(solution)/shard_map/all_gather | solution.py:25
  166.5 11.6 %fusion.14 = (bf16[4096,1024]{1,0:T(8,128)(2,1)}, bf16[4096,1024]{1,0:T(8,128)(2,1)}) fusion(bf16[8192,1024]{1,0:T(8,128)(2,1)} %all-gather.3.cloned.1.call-done), kind=kLoop, calls=%fused_computation.29 | loop fusion | bytes 33554432 | tf_op jit(solution)/shard_map/jit(_take)/gather | solution.py:27
  178.2 11.3 %copy.7 = bf16[4096,1024]{0,1:T(8,128)(2,1)} copy(bf16[4096,1024]{1,0:T(8,128)(2,1)} %get-tuple-element.5) | data formatting | bytes 16777216 | tf_op jit(solution)/shard_map/jit(_take)/gather | solution.py:27
  189.5 11.8 %copy.8 = bf16[4096,1024]{0,1:T(8,128)(2,1)} copy(bf16[4096,1024]{1,0:T(8,128)(2,1)} %get-tuple-element.6) | data formatting | bytes 16777216 | tf_op jit(solution)/shard_map/jit(_take)/gather | solution.py:27
  201.3 6.1 %gather_fusion = bf16[4,4096,128]{1,2,0:T(8,128)(2,1)} fusion(bf16[4096,8,128]{0,2,1:T(8,128)(2,1)} %bitcast.24, s32[1024]{0:T(1024)S(1)} %pad_clamp_fusion.1), kind=kCustom, calls=%fused_computation | custom fusion | bytes 8388624 | tf_op jit(solution)/shard_map/jit(_take)/gather | solution.py:27
  207.4 6.2 %gather_fusion.1 = bf16[4,4096,128]{1,2,0:T(8,128)(2,1)} fusion(bf16[4096,8,128]{0,2,1:T(8,128)(2,1)} %bitcast.25, s32[1024]{0:T(1024)S(1)} %pad_clamp_fusion.1), kind=kCustom, calls=%fused_computation.1 | custom fusion | bytes 8388624 | tf_op jit(solution)/shard_map/jit(_take)/gather | solution.py:27
  213.6 8.1 %fusion.9 = f32[1,1,4,128,128]{4,3,2,1,0:T(8,128)} fusion(bf16[4096,4,128]{0,2,1:T(8,128)(2,1)} %bitcast.29, bf16[4096,4,128]{0,2,1:T(8,128)(2,1)} %bitcast.28, pred[4]{0:T(512)(128)(4,1)S(1)} %get-tuple-element.9, bf16[4096,4,128]{0,2,1:T(8,128)(2,1)} %bitcast.31, bf16[4096,4,128]{0,2,1:T(8,128)(2,1)} %bitcast.30, pred[4]{0:T(512)(128)(4,1)S(1)} %get-tuple-element.10, ...), kind=kOutput, calls=%fused_computation.15 | convolution fusion | flops 1115750400 | bytes 17039372 | tf_op jit(solution)/shard_map/nbi,nbj->bij/dot_general | solution.py:13
  (3 shorter events, 0.0 us)
Async XLA Ops:
  6.5 57.0 %all-gather.5.cloned.1.call-start = ((), (), s32[]{:S(2)}) async-start(), calls=%async_computation.1 | async-start | bytes 5242880 | tf_op jit(solution)/shard_map/all_gather | solution.py:24
  7.3 159.3 %all-gather.3.cloned.1.call-start = ((), (), s32[]{:S(2)}) async-start(), calls=%async_computation | async-start | bytes 17039360 | tf_op jit(solution)/shard_map/all_gather | solution.py:25
Sparse Core Ops, SparseCore 0:
  9.1 54.3 all-gather.4
  66.3 100.2 all-gather.2
where the time goes:
time: 229 us
  waiting for transfers between devices  138 us (60%)
  local copies, waits for them, and re-layouts  65.8 us (29%)
  between operations  14.1 us (6%)
  matrix products  8.1 us (4%)
    all_gather x1, waiting for transfers between devices, on_device(): piece = lax.all_gather(activations, 'out', axis=0, tiled=True)  84.2 us
    all_gather x1, waiting for transfers between devices, on_device(): grad_all = lax.all_gather(out_grad, 'in', axis=0, tiled=True)  52.8 us
    gather x5, local copies, waits for them, and re-layouts, on_device(): left = jnp.take(piece.reshape(height, tile_rows, BLK), local_rows, axis=1)  47 us
    gather x5, local copies, waits for them, and re-layouts, block_products(): jnp.take(grad_rows.reshape(width, tile_cols, BLK), local_cols, axis=1)  18.8 us
    dot_general x1, matrix products, block_products(): jnp.einsum('nbi,nbj->bij', left_rows, right, preferred_element_type=jnp.f...  8.1 us
  transfers between devices with their start and end apart: 2, of which 2 were waited for; matrix products, arithmetic and copies ran while one was open for 9% of the time, Pallas kernels for 0%

commit v1 on v0

--- a/solution.py
+++ b/solution.py
@@ -1,3 +1,4 @@
+import functools
 import jax
 import jax.numpy as jnp
 from jax import lax
@@ -5,6 +6,19 @@
 
 BLK = 128
 MAXB = 4
+
+
+def create_tasks(block_in, array_axis):
+    g_now = jnp.concatenate(
+        lax.all_to_all(
+            jnp.stack(lax.axis_size("out") * [block_in]), "out", split_axis=0, concat_axis=0
+        ),
+        axis=array_axis,
+    )
+    return g_now
+
+
+launch_scales_over_axis = functools.partial(create_tasks, array_axis=0)
 
 
 def block_products(left_rows, grad_rows, local_cols, tile_cols):
@@ -22,7 +36,7 @@
     local_cols = block_cols[0, 0] - out_place * tile_cols
     live = counts[0, 0]
     grad_all = lax.all_gather(out_grad, "in", axis=0, tiled=True)
-    piece = lax.all_gather(activations, "out", axis=0, tiled=True)
+    piece = launch_scales_over_axis(activations)
     height = piece.shape[0]
     left = jnp.take(piece.reshape(height, tile_rows, BLK), local_rows, axis=1)
     totals = block_products(left, grad_all, local_cols, tile_cols)

time: 229 us -> 488 us (2.13); the launches traced: 229 us -> 479 us
  waiting for transfers between devices: 138 us -> 343 us
  local copies, waits for them, and re-layouts: 65.8 us -> 100 us
  starting transfers between devices: 0.04 us -> 13.5 us
    all_to_all x0 -> x1, waiting for transfers between devices: none -> 290 us  [create_tasks(): lax.all_to_all(jnp.stack(lax.axis_size('out') * [block_in]), 'out', split...]
    all_gather x1 -> x0, waiting for transfers between devices: 84.2 us -> none  [on_device(): piece = lax.all_gather(activations, 'out', axis=0, tiled=True)]
    gather x5 -> x7, local copies, waits for them, and re-layouts: 47 us -> 74.4 us  [on_device(): left = jnp.take(piece.reshape(height, tile_rows, BLK), local_rows, axis=1)]
    all_to_all x0 -> x1, starting transfers between devices: none -> 13.5 us  [create_tasks(): lax.all_to_all(jnp.stack(lax.axis_size('out') * [block_in]), 'out', split...]
    another operation x0 -> x1, local copies, waits for them, and re-layouts: none -> 6.2 us  [create_tasks(): jnp.stack(lax.axis_size('out') * [block_in])]
  transfers between devices with their start and end apart: 2 -> 2, of which waited for: 2 -> 2; matrix products, arithmetic and copies ran while one was open for 9% -> 4% of each run, Pallas kernels for 0% -> 0%
where the time goes in v1:
time: 488 us; the launch traced here: 479 us
  waiting for transfers between devices  343 us (70%)
  local copies, waits for them, and re-layouts  100 us (20%)
  between operations  14.1 us (3%)
  starting transfers between devices  13.5 us (3%)
  matrix products  8.1 us (2%)
    all_to_all x1, waiting for transfers between devices, create_tasks(): lax.all_to_all(jnp.stack(lax.axis_size('out') * [block_in]), 'out', split...  290 us
    gather x7, local copies, waits for them, and re-layouts, on_device(): left = jnp.take(piece.reshape(height, tile_rows, BLK), local_rows, axis=1)  74.4 us
    all_gather x1, waiting for transfers between devices, on_device(): grad_all = lax.all_gather(out_grad, 'in', axis=0, tiled=True)  52.7 us
    gather x5, local copies, waits for them, and re-layouts, block_products(): jnp.take(grad_rows.reshape(width, tile_cols, BLK), local_cols, axis=1)  18.7 us
    all_to_all x1, starting transfers between devices, create_tasks(): lax.all_to_all(jnp.stack(lax.axis_size('out') * [block_in]), 'out', split...  13.5 us
  transfers between devices with their start and end apart: 2, of which 2 were waited for; matrix products, arithmetic and copies ran while one was open for 4% of the time, Pallas kernels for 0%

profile of v1, /device:TPU:1, one launch (start us, length us, event | category | flops | bytes accessed | tf_op | source)
XLA Modules:
  0.0 479.3 jit_solution(12984525636216984914)
XLA Ops:
  6.5 1.1 copy.11
  7.7 6.2 %stack.2 = bf16[64,128,1024]{1,2,0:T(8,128)(2,1)} broadcast(bf16[128,1024]{0,1:T(8,128)(2,1)S(1)} %copy.11), dimensions={1,2} | broadcast | bytes 17039360 | tf_op jit(solution)/shard_map/stack | solution.py:14
  13.9 0.0 copy-start.1
  13.9 0.0 copy-start
  13.9 13.5 %all-to-all-start = ((bf16[64,128,1024]{1,2,0:T(8,128)(2,1)}), bf16[64,128,1024]{1,2,0:T(8,128)(2,1)}, u32[]{:S(2)}, u32[]{:S(2)}) async-start(bf16[64,128,1024]{1,2,0:T(8,128)(2,1)} %stack.2), calls=%async_computation | async-start | bytes 33554432 | tf_op jit(solution)/shard_map/all_to_all | solution.py:13
  27.3 0.0 all-gather.2.cloned.1.call-start
  27.4 0.7 all-gather.2.cloned.1.call-update
  28.7 0.0 copy-done.1
  28.8 0.0 copy-done
  28.8 52.7 %all-gather.2.cloned.1.call-done = bf16[8192,256]{1,0:T(8,128)(2,1)} async-done(((bf16[2048,256]{1,0:T(8,128)(2,1)}), bf16[8192,256]{1,0:T(8,128)(2,1)}) %all-gather.2.cloned.1.call-update) | async-done | bytes 4194320 | tf_op jit(solution)/shard_map/all_gather | solution.py:38
  81.5 4.4 fusion.15
  85.9 2.9 copy.14
  88.8 4.1 copy.15
  92.9 2.8 gather_fusion.2
  95.7 4.5 gather_fusion.3
  100.2 289.7 %all-to-all-done = bf16[64,128,1024]{1,2,0:T(8,128)(2,1)} async-done(((bf16[64,128,1024]{1,2,0:T(8,128)(2,1)}), bf16[64,128,1024]{1,2,0:T(8,128)(2,1)}, u32[]{:S(2)}, u32[]{:S(2)}) %all-to-all-start) | async-done | bytes 16777248 | tf_op jit(solution)/shard_map/all_to_all | solution.py:13
  389.9 11.5 %fusion.14 = (bf16[32,128,1024]{1,2,0:T(8,128)(2,1)}, bf16[32,128,1024]{1,2,0:T(8,128)(2,1)}) fusion(bf16[64,128,1024]{1,2,0:T(8,128)(2,1)} %all-to-all-done), kind=kLoop, calls=%fused_computation.29 | loop fusion | bytes 33554432 | tf_op jit(solution)/shard_map/jit(_take)/gather | solution.py:41
  401.4 12.0 %copy.12 = bf16[32,128,1024]{1,0,2:T(8,128)(2,1)} copy(bf16[32,128,1024]{1,2,0:T(8,128)(2,1)} %get-tuple-element.5) | data formatting | bytes 16777216 | tf_op jit(solution)/shard_map/jit(_take)/gather | solution.py:41
  413.4 13.3 %reshape.72 = bf16[4096,8,128]{0,2,1:T(8,128)(2,1)} reshape(bf16[32,128,1024]{1,0,2:T(8,128)(2,1)} %copy.12) | data formatting | bytes 16777216 | tf_op jit(solution)/shard_map/jit(_take)/gather | solution.py:41
  426.7 12.0 %copy.13 = bf16[32,128,1024]{1,0,2:T(8,128)(2,1)} copy(bf16[32,128,1024]{1,2,0:T(8,128)(2,1)} %get-tuple-element.6) | data formatting | bytes 16777216 | tf_op jit(solution)/shard_map/jit(_take)/gather | solution.py:41
  438.7 13.3 %reshape.73 = bf16[4096,8,128]{0,2,1:T(8,128)(2,1)} reshape(bf16[32,128,1024]{1,0,2:T(8,128)(2,1)} %copy.13) | data formatting | bytes 16777216 | tf_op jit(solution)/shard_map/jit(_take)/gather | solution.py:41
  452.0 6.1 %gather_fusion = bf16[4,4096,128]{1,2,0:T(8,128)(2,1)} fusion(bf16[4096,8,128]{0,2,1:T(8,128)(2,1)} %reshape.72, s32[1024]{0:T(1024)S(1)} %pad_clamp_fusion.1), kind=kCustom, calls=%fused_computation | custom fusion | bytes 8388624 | tf_op jit(solution)/shard_map/jit(_take)/gather | solution.py:41
  458.2 6.1 %gather_fusion.1 = bf16[4,4096,128]{1,2,0:T(8,128)(2,1)} fusion(bf16[4096,8,128]{0,2,1:T(8,128)(2,1)} %reshape.73, s32[1024]{0:T(1024)S(1)} %pad_clamp_fusion.1), kind=kCustom, calls=%fused_computation.1 | custom fusion | bytes 8388624 | tf_op jit(solution)/shard_map/jit(_take)/gather | solution.py:41
  464.3 8.1 %fusion.9 = f32[1,1,4,128,128]{4,3,2,1,0:T(8,128)} fusion(bf16[4096,4,128]{0,2,1:T(8,128)(2,1)} %bitcast.29, bf16[4096,4,128]{0,2,1:T(8,128)(2,1)} %bitcast.28, pred[4]{0:T(512)(128)(4,1)S(1)} %get-tuple-element.9, bf16[4096,4,128]{0,2,1:T(8,128)(2,1)} %bitcast.31, bf16[4096,4,128]{0,2,1:T(8,128)(2,1)} %bitcast.30, pred[4]{0:T(512)(128)(4,1)S(1)} %get-tuple-element.10, ...), kind=kOutput, calls=%fused_computation.15 | convolution fusion | flops 1115750400 | bytes 17039372 | tf_op jit(solution)/shard_map/nbi,nbj->bij/dot_general | solution.py:27
  (6 shorter events, 0.0 us)
Async XLA Ops:
  13.9 14.9 %copy-start.1 = (s32[1,1,4]{2,1,0:T(1,128)S(1)}, s32[1,1,4]{2,1,0:T(1,128)}, u32[]{:S(2)}) copy-start(s32[1,1,4]{2,1,0:T(1,128)} %param.7) | copy-start | bytes 52
  13.9 14.9 %copy-start = (s32[1,1,4]{2,1,0:T(1,128)S(1)}, s32[1,1,4]{2,1,0:T(1,128)}, u32[]{:S(2)}) copy-start(s32[1,1,4]{2,1,0:T(1,128)} %param.8) | copy-start | bytes 52
  13.9 376.0 %all-to-all-start = ((bf16[64,128,1024]{1,2,0:T(8,128)(2,1)}), bf16[64,128,1024]{1,2,0:T(8,128)(2,1)}, u32[]{:S(2)}, u32[]{:S(2)}) async-start(bf16[64,128,1024]{1,2,0:T(8,128)(2,1)} %stack.2), calls=%async_computation | async-start | bytes 33554432 | tf_op jit(solution)/shard_map/all_to_all | solution.py:13
  27.3 54.2 %all-gather.2.cloned.1.call-start = ((), (), s32[]{:S(2)}) async-start(), calls=%async_computation.1 | async-start | bytes 5242880 | tf_op jit(solution)/shard_map/all_gather | solution.py:38
Sparse Core Ops, SparseCore 0:
  30.0 51.4 all-gather.1
